TPU v7x, 32 devices: a whole 2x2x4 slice. The times are simulated.
32 devices in a mesh: dp: 2 (over x), mp: 16 (over z, y, core).
Axes of the slice: x: 2, y: 2, z: 4, core: 2. Of those that a mesh axis runs over, the one named last changes fastest.
Arguments:
- inputs: bfloat16 [256, 8192], P('dp', 'mp'), may hold values from -6 to 6
- out_grad: bfloat16 [256, 8192], P('dp', 'mp'), may hold values from -6 to 6
- w_in: bfloat16 [128, 4, 128, 128], P('mp'), may hold values from -0.25 to 0.25
- in_blocks: int32 [128, 4], P('mp'), may hold values from 0 to 63, as said below
- w_out: bfloat16 [128, 4, 128, 128], P('mp'), may hold values from -0.1875 to 0.1875
- out_blocks: int32 [128, 4], P('mp'), may hold values from 0 to 63, as said below
Outputs:
- outputs: bfloat16 [256, 8192], P('dp', 'mp')
- in_grad: bfloat16 [256, 8192], P('dp', 'mp')
- w_in_grad: bfloat16 [128, 4, 128, 128], P('mp')
- w_out_grad: bfloat16 [128, 4, 128, 128], P('mp')
Inputs may be any that keep to these rules, and one draw needn't show every extreme that they name: `in_blocks`: the 4 input column blocks of one hidden block row are distinct. `out_blocks`: the 4 output column blocks of one hidden block row are distinct.
All inputs are finite; a program needn't handle non-finite values.
Results may differ from a plain program's by a relative error of at most 0.017.
Values may be sent and summed in bfloat16 or wider, within the bound.
No kernel may reach another device: no remote copies, remote signals or barrier semaphores. Data moves between devices by JAX's collectives and lax.ppermute only.
A program may use at most 64 MiB of HBM per device.

v0:
```python
import jax
import jax.numpy as jnp
from jax import lax
from jax.sharding import PartitionSpec as P

root_half = 0.7071067811865476
inv_root_two_pi = 0.3989422804014327


def gelu_value(preact):
    return 0.5 * preact * (1.0 + jax.scipy.special.erf(preact * root_half))


def gelu_slope(preact):
    return (
        0.5 * (1.0 + jax.scipy.special.erf(preact * root_half))
        + preact * jnp.exp(-0.5 * preact * preact) * inv_root_two_pi
    )


def per_device(inputs, out_grad, w_in, in_blocks, w_out, out_blocks):
    tok_rows = inputs.shape[0]
    hid_rows = w_in.shape[0]
    per_row = w_in.shape[1]
    block_size = w_in.shape[2]
    pair_count = hid_rows * per_row
    owners = lax.axis_size("mp")
    in_full, grad_full = (
        lax.all_gather(inputs, "mp", axis=1, tiled=True),
        lax.all_gather(out_grad, "mp", axis=1, tiled=True),
    )
    col_count = in_full.shape[1] // block_size
    in_flat = in_blocks.reshape(pair_count)
    out_flat = out_blocks.reshape(pair_count)
    empty = jnp.zeros((tok_rows, col_count, block_size), jnp.float32)
    in_sel = jnp.take(in_full.reshape(tok_rows, col_count, block_size), in_flat, axis=1)
    in_sel = in_sel.reshape(tok_rows, hid_rows, per_row, block_size)
    preact = jnp.einsum("trki,rkio->tro", in_sel, w_in, preferred_element_type=jnp.float32)
    hidden = gelu_value(preact).astype(jnp.bfloat16)
    out_terms = jnp.einsum("tri,rkio->trko", hidden, w_out, preferred_element_type=jnp.float32)
    out_terms = out_terms.reshape(tok_rows, pair_count, block_size)
    out_local = empty.at[:, out_flat].add(out_terms)
    out_local = out_local.reshape(tok_rows, col_count * block_size)

    def collect(received):
        return received.reshape(owners, tok_rows, -1).sum(axis=0).astype(jnp.bfloat16)

    outputs = collect(lax.all_to_all(out_local, "mp", split_axis=1, concat_axis=0, tiled=True))
    grad_sel = jnp.take(grad_full.reshape(tok_rows, col_count, block_size), out_flat, axis=1)
    grad_sel = grad_sel.reshape(tok_rows, hid_rows, per_row, block_size)
    hid_grad = jnp.einsum("trko,rkio->tri", grad_sel, w_out, preferred_element_type=jnp.float32)
    pre_grad = (hid_grad * gelu_slope(preact)).astype(jnp.bfloat16)
    in_terms = jnp.einsum("tro,rkio->trki", pre_grad, w_in, preferred_element_type=jnp.float32)
    in_terms = in_terms.reshape(tok_rows, pair_count, block_size)
    in_local = empty.at[:, in_flat].add(in_terms)
    in_local = in_local.reshape(tok_rows, col_count * block_size)
    w_in_part = jnp.einsum("trki,tro->rkio", in_sel, pre_grad, preferred_element_type=jnp.float32)
    in_grad = collect(lax.all_to_all(in_local, "mp", split_axis=1, concat_axis=0, tiled=True))
    w_out_part = jnp.einsum("tri,trko->rkio", hidden, grad_sel, preferred_element_type=jnp.float32)
    w_in_total, w_out_total = (
        lax.psum(w_in_part.astype(jnp.bfloat16), "dp").astype(jnp.float32),
        lax.psum(w_out_part.astype(jnp.bfloat16), "dp").astype(jnp.float32),
    )
    w_in_grad = w_in_total.astype(jnp.bfloat16)
    w_out_grad = w_out_total.astype(jnp.bfloat16)
    return (outputs, in_grad, w_in_grad, w_out_grad)


def solution(mesh):
    return jax.shard_map(
        per_device,
        mesh=mesh,
        in_specs=(
            P("dp", "mp"),
            P("dp", "mp"),
            P("mp", None, None, None),
            P("mp", None),
            P("mp", None, None, None),
            P("mp", None),
        ),
        out_specs=(
            P("dp", "mp"),
            P("dp", "mp"),
            P("mp", None, None, None),
            P("mp", None, None, None),
        ),
        check_vma=False,
    )
```

profile of v0, /device:TPU:13, one launch (start us, length us, event | category | flops | bytes accessed | tf_op | source)
XLA Modules:
  0.0 331.5 jit_solution(15757751601421945742)
XLA Ops:
  7.2 1.7 copy.43
  9.0 1.7 copy.48
  11.7 0.8 copy.41
  12.6 39.3 %all-gather.3.cloned.1.call-done = bf16[128,8192]{0,1:T(8,128)(2,1)} async-done(((bf16[128,512]{0,1:T(8,128)(2,1)}), bf16[128,8192]{0,1:T(8,128)(2,1)}) %all-gather.3.cloned.1.call-update) | async-done | bytes 2097168 | tf_op jit(solution)/shard_map/all_gather | solution.py:29
  51.8 3.2 copy.44
  55.1 39.7 %all-gather.5.cloned.1.call-done = bf16[128,8192]{0,1:T(8,128)(2,1)} async-done(((bf16[128,512]{0,1:T(8,128)(2,1)}), bf16[128,8192]{0,1:T(8,128)(2,1)}) %all-gather.5.cloned.1.call-update) | async-done | bytes 2097168 | tf_op jit(solution)/shard_map/all_gather | solution.py:30
  94.8 4.1 %copy.49 = bf16[128,64,128]{2,0,1:T(8,128)(2,1)} copy(bf16[128,64,128]{0,2,1:T(8,128)(2,1)} %bitcast.71) | data formatting | bytes 4194304 | tf_op jit(solution)/shard_map/reshape | solution.py:49
  98.8 1.6 gather_fusion
  100.5 1.4 broadcast_select_fusion.1
  102.3 3.2 gather_fusion.1
  105.6 1.5 broadcast_select_fusion
  107.6 1.8 fusion.14
  109.3 2.4 broadcast_in_dim.14.clone.1
  111.8 7.1 %scatter_fusion.1 = f32[128,64,128]{2,0,1:T(8,128)} fusion(f32[128,64,128]{2,0,1:T(8,128)} %broadcast_in_dim.14.clone.1, s32[32]{0:T(128)S(1)} %fusion.10, f32[32,128,128]{2,1,0:T(8,128)} %bitcast.67), kind=kCustom, calls=%fused_computation.3 | custom fusion | flops 524288 | bytes 6291584 | tf_op jit(solution)/shard_map/scatter-add | solution.py:55
  118.8 5.6 %copy.50 = f32[128,64,128]{0,2,1:T(8,128)} copy(f32[128,64,128]{2,0,1:T(8,128)} %scatter_fusion.1) | data formatting | bytes 8388608 | tf_op jit(solution)/shard_map/scatter-add | solution.py:55
  124.5 6.5 %all-to-all-start.1 = ((f32[128,16,512]{0,2,1:T(8,128)}), f32[128,16,512]{0,2,1:T(8,128)}, u32[]{:S(2)}, u32[]{:S(2)}) async-start(f32[128,16,512]{0,2,1:T(8,128)} %bitcast.63), calls=%async_computation.1 | async-start | bytes 8388608 | tf_op jit(solution)/shard_map/all_to_all | solution.py:58
  131.1 3.0 fusion.12
  134.1 2.5 broadcast_in_dim.14.clone
  136.6 7.0 %scatter_fusion = f32[128,64,128]{2,0,1:T(8,128)} fusion(f32[128,64,128]{2,0,1:T(8,128)} %broadcast_in_dim.14.clone, s32[32]{0:T(128)S(1)} %fusion.9, f32[32,128,128]{2,1,0:T(8,128)} %bitcast.66), kind=kCustom, calls=%fused_computation.2 | custom fusion | flops 524288 | bytes 6291584 | tf_op jit(solution)/shard_map/scatter-add | solution.py:42
  143.6 5.6 %copy.45 = f32[128,64,128]{0,2,1:T(8,128)} copy(f32[128,64,128]{2,0,1:T(8,128)} %scatter_fusion) | data formatting | bytes 8388608 | tf_op jit(solution)/shard_map/scatter-add | solution.py:42
  149.2 74.3 %all-to-all-done.1 = f32[128,16,512]{0,2,1:T(8,128)} async-done(((f32[128,16,512]{0,2,1:T(8,128)}), f32[128,16,512]{0,2,1:T(8,128)}, u32[]{:S(2)}, u32[]{:S(2)}) %all-to-all-start.1) | async-done | bytes 4194336 | tf_op jit(solution)/shard_map/all_to_all | solution.py:58
  223.5 4.9 %all-to-all-start = ((f32[128,16,512]{0,2,1:T(8,128)}), f32[128,16,512]{0,2,1:T(8,128)}, u32[]{:S(2)}, u32[]{:S(2)}) async-start(f32[128,16,512]{0,2,1:T(8,128)} %bitcast.62), calls=%async_computation | async-start | bytes 8388608 | tf_op jit(solution)/shard_map/all_to_all | solution.py:48
  228.4 1.5 convolution_convert_fusion.1
  229.9 1.5 fusion
  231.4 64.4 %all-reduce.3.cloned.1.call-done = (bf16[8,4,128,128]{3,2,1,0:T(8,128)(2,1)}, bf16[8,4,128,128]{2,3,1,0:T(8,128)(2,1)}) async-done(((bf16[8,4,128,128]{3,2,1,0:T(8,128)(2,1)}, bf16[8,4,128,128]{2,3,1,0:T(8,128)(2,1)}), (bf16[8,4,128,128]{3,2,1,0:T(8,128)(2,1)}, bf16[8,4,128,128]{2,3,1,0:T(8,128)(2,1)})) %all-reduce.3.cloned.1.call-update) | async-done | bytes 2097168 | tf_op jit(solution)/shard_map/psum | solution.py:61
  295.8 2.3 copy.55
  298.1 2.4 reduce_sum.19
  300.5 0.8 copy.54
  301.2 19.6 %all-to-all-done = f32[128,16,512]{0,2,1:T(8,128)} async-done(((f32[128,16,512]{0,2,1:T(8,128)}), f32[128,16,512]{0,2,1:T(8,128)}, u32[]{:S(2)}, u32[]{:S(2)}) %all-to-all-start) | async-done | bytes 4194336 | tf_op jit(solution)/shard_map/all_to_all | solution.py:48
  320.8 2.4 reduce_sum.18
  323.2 0.8 copy.53
  324.0 1.0 copy.68
  (31 shorter events, 2.2 us)
Async XLA Ops:
  7.2 94.7 %copy-start = (bf16[8,4,128,128]{3,2,1,0:T(8,128)(2,1)S(1)}, bf16[8,4,128,128]{3,2,1,0:T(8,128)(2,1)}, u32[]{:S(2)}) copy-start(bf16[8,4,128,128]{3,2,1,0:T(8,128)(2,1)} %param.10) | copy-start | bytes 3145732
  7.2 44.7 %all-gather.3.cloned.1.call-start = ((), (), s32[]{:S(2)}) async-start(), calls=%async_computation.2 | async-start | bytes 2228224 | tf_op jit(solution)/shard_map/all_gather | solution.py:29
  9.0 85.8 %all-gather.5.cloned.1.call-start = ((), (), s32[]{:S(2)}) async-start(), calls=%async_computation.3 | async-start | bytes 2228224 | tf_op jit(solution)/shard_map/all_gather | solution.py:30
  105.6 1.5 copy-start.3
  107.0 2.3 copy-start.1
  124.5 99.0 %all-to-all-start.1 = ((f32[128,16,512]{0,2,1:T(8,128)}), f32[128,16,512]{0,2,1:T(8,128)}, u32[]{:S(2)}, u32[]{:S(2)}) async-start(f32[128,16,512]{0,2,1:T(8,128)} %bitcast.63), calls=%async_computation.1 | async-start | bytes 8388608 | tf_op jit(solution)/shard_map/all_to_all | solution.py:58
  223.5 97.4 %all-to-all-start = ((f32[128,16,512]{0,2,1:T(8,128)}), f32[128,16,512]{0,2,1:T(8,128)}, u32[]{:S(2)}, u32[]{:S(2)}) async-start(f32[128,16,512]{0,2,1:T(8,128)} %bitcast.62), calls=%async_computation | async-start | bytes 8388608 | tf_op jit(solution)/shard_map/all_to_all | solution.py:48
  228.4 67.4 %all-reduce.3.cloned.1.call-start = ((), (), s32[]{:S(2)}) async-start(), calls=%async_computation.4 | async-start | bytes 4194304 | tf_op jit(solution)/shard_map/psum | solution.py:61
  228.4 1.5 copy-start.2
  301.2 22.8 %copy-start.4 = (bf16[8,4,128,128]{3,2,1,0:T(8,128)(2,1)S(1)}, bf16[8,4,128,128]{3,2,1,0:T(8,128)(2,1)}, u32[]{:S(2)}) copy-start(bf16[8,4,128,128]{3,2,1,0:T(8,128)(2,1)} %get-tuple-element.25) | copy-start | bytes 3145732
Sparse Core Ops, SparseCore 0:
  10.7 41.0 all-gather.2
  54.6 40.1 all-gather.4
  232.1 63.6 all-reduce.2
where the time goes:
time: 333 us; the launch traced here: 332 us
  waiting for transfers between devices  237 us (71%)
  local copies, waits for them, and re-layouts  38.4 us (12%)
  other arithmetic  21.8 us (7%)
  between operations  13.9 us (4%)
  starting transfers between devices  11.5 us (3%)
  matrix products  8.61 us (3%)
    all_to_all x1, waiting for transfers between devices, per_device(): lax.all_to_all(in_local, 'mp', split_axis=1, concat_axis=0, tiled=True)  74.3 us
    psum x1, waiting for transfers between devices, per_device(): lax.psum(w_in_part.astype(jnp.bfloat16), 'dp').astype(jnp.float32)  64.4 us
    all_gather x1, waiting for transfers between devices, per_device(): lax.all_gather(out_grad, 'mp', axis=1, tiled=True)  39.7 us
    all_gather x1, waiting for transfers between devices, per_device(): lax.all_gather(inputs, 'mp', axis=1, tiled=True)  39.3 us
    all_to_all x1, waiting for transfers between devices, per_device(): lax.all_to_all(out_local, 'mp', split_axis=1, concat_axis=0, tiled=True)  19.6 us
    unnamed x18, local copies, waits for them, and re-layouts  9.78 us
    scatter-add x1, other arithmetic, per_device(): in_local = empty.at[:, in_flat].add(in_terms)  7.07 us
    scatter-add x1, other arithmetic, per_device(): out_local = empty.at[:, out_flat].add(out_terms)  7.02 us
  transfers between devices with their start and end apart: 5, of which 5 were waited for; matrix products, arithmetic and copies ran while one was open for 10% of the time, Pallas kernels for 0%

commit v1 on v0

--- a/solution.py
+++ b/solution.py
@@ -5,6 +5,14 @@
 
 root_half = 0.7071067811865476
 inv_root_two_pi = 0.3989422804014327
+
+
+def rest_the_weights(axis_tag, base_x):
+    s_next = lax.axis_size(axis_tag)
+    far_arr = jnp.split(base_x, s_next, axis=1)
+    z1 = jnp.stack(far_arr)
+    met_up = lax.all_to_all(z1, axis_tag, 0, 0)
+    return jnp.concatenate(met_up, axis=0)
 
 
 def gelu_value(preact):
@@ -55,7 +63,7 @@
     in_local = empty.at[:, in_flat].add(in_terms)
     in_local = in_local.reshape(tok_rows, col_count * block_size)
     w_in_part = jnp.einsum("trki,tro->rkio", in_sel, pre_grad, preferred_element_type=jnp.float32)
-    in_grad = collect(lax.all_to_all(in_local, "mp", split_axis=1, concat_axis=0, tiled=True))
+    in_grad = collect(rest_the_weights("mp", in_local))
     w_out_part = jnp.einsum("tri,trko->rkio", hidden, grad_sel, preferred_element_type=jnp.float32)
     w_in_total, w_out_total = (
         lax.psum(w_in_part.astype(jnp.bfloat16), "dp").astype(jnp.float32),

time: 333 us -> 290 us (0.87)
  waiting for transfers between devices: 237 us -> 173 us
  local copies, waits for them, and re-layouts: 38.4 us -> 58.6 us
    all_to_all x1, waiting for transfers between devices: 74.3 us -> 18.9 us  [rest_the_weights(): met_up = lax.all_to_all(z1, axis_tag, 0, 0)]
    unnamed x18 -> x33, local copies, waits for them, and re-layouts: 9.78 us -> 29.3 us
    all_gather x1, waiting for transfers between devices: 39.7 us -> 30.4 us  [per_device(): lax.all_gather(out_grad, 'mp', axis=1, tiled=True)]
  transfers between devices with their start and end apart: 5 -> 5, of which waited for: 5 -> 5; matrix products, arithmetic and copies ran while one was open for 10% -> 29% of each run, Pallas kernels for 0% -> 0%
where the time goes in v1:
time: 290 us; the launch traced here: 289 us
  waiting for transfers between devices  173 us (60%)
  local copies, waits for them, and re-layouts  58.6 us (20%)
  other arithmetic  21.8 us (8%)
  between operations  13.9 us (5%)
  starting transfers between devices  11.8 us (4%)
  matrix products  9.86 us (3%)
    psum x1, waiting for transfers between devices, per_device(): lax.psum(w_in_part.astype(jnp.bfloat16), 'dp').astype(jnp.float32)  63.8 us
    all_gather x1, waiting for transfers between devices, per_device(): lax.all_gather(inputs, 'mp', axis=1, tiled=True)  39.4 us
    all_gather x1, waiting for transfers between devices, per_device(): lax.all_gather(out_grad, 'mp', axis=1, tiled=True)  30.4 us
    unnamed x33, local copies, waits for them, and re-layouts  29.3 us
    all_to_all x1, waiting for transfers between devices, per_device(): lax.all_to_all(out_local, 'mp', split_axis=1, concat_axis=0, tiled=True)  20.8 us
    all_to_all x1, waiting for transfers between devices, rest_the_weights(): met_up = lax.all_to_all(z1, axis_tag, 0, 0)  18.9 us
    scatter-add x1, other arithmetic, per_device(): out_local = empty.at[:, out_flat].add(out_terms)  7.01 us
    scatter-add x1, other arithmetic, per_device(): in_local = empty.at[:, in_flat].add(in_terms)  7.01 us
  transfers between devices with their start and end apart: 5, of which 5 were waited for; matrix products, arithmetic and copies ran while one was open for 29% of the time, Pallas kernels for 0%

profile of v1, /device:TPU:13, one launch (start us, length us, event | category | flops | bytes accessed | tf_op | source)
XLA Modules:
  0.0 289.2 jit_solution(16791270860914510880)
XLA Ops:
  7.2 1.7 copy.43
  9.0 1.7 copy.48
  12.5 39.4 %all-gather.3.cloned.1.call-done = bf16[128,8192]{0,1:T(8,128)(2,1)} async-done(((bf16[128,512]{0,1:T(8,128)(2,1)}), bf16[128,8192]{0,1:T(8,128)(2,1)}) %all-gather.3.cloned.1.call-update) | async-done | bytes 2097168 | tf_op jit(solution)/shard_map/all_gather | solution.py:37
  51.8 3.2 %copy.44 = bf16[128,64,128]{2,0,1:T(8,128)(2,1)S(1)} copy(bf16[128,64,128]{0,2,1:T(8,128)(2,1)} %bitcast.150) | data formatting | bytes 4194304 | tf_op jit(solution)/shard_map/reshape | solution.py:44
  59.8 1.7 fusion.28
  61.5 2.4 broadcast_in_dim.14.clone
  64.0 7.0 %scatter_fusion = f32[128,64,128]{2,0,1:T(8,128)} fusion(f32[128,64,128]{2,0,1:T(8,128)} %broadcast_in_dim.14.clone, s32[32]{0:T(128)S(1)} %fusion.25, f32[32,128,128]{2,1,0:T(8,128)} %bitcast.145), kind=kCustom, calls=%fused_computation.2 | custom fusion | flops 524288 | bytes 6291584 | tf_op jit(solution)/shard_map/scatter-add | solution.py:50
  71.0 5.6 %copy.45 = f32[128,64,128]{0,2,1:T(8,128)} copy(f32[128,64,128]{2,0,1:T(8,128)} %scatter_fusion) | data formatting | bytes 8388608 | tf_op jit(solution)/shard_map/scatter-add | solution.py:50
  76.6 6.7 %all-to-all-start = ((f32[128,16,512]{0,2,1:T(8,128)}), f32[128,16,512]{0,2,1:T(8,128)}, u32[]{:S(2)}, u32[]{:S(2)}) async-start(f32[128,16,512]{0,2,1:T(8,128)} %bitcast.142), calls=%async_computation | async-start | bytes 8388608 | tf_op jit(solution)/shard_map/all_to_all | solution.py:56
  83.5 30.4 %all-gather.5.cloned.1.call-done = bf16[128,8192]{0,1:T(8,128)(2,1)} async-done(((bf16[128,512]{0,1:T(8,128)(2,1)}), bf16[128,8192]{0,1:T(8,128)(2,1)}) %all-gather.5.cloned.1.call-update) | async-done | bytes 2097168 | tf_op jit(solution)/shard_map/all_gather | solution.py:38
  113.9 4.1 %copy.49 = bf16[128,64,128]{2,0,1:T(8,128)(2,1)} copy(bf16[128,64,128]{0,2,1:T(8,128)(2,1)} %bitcast.149) | data formatting | bytes 4194304 | tf_op jit(solution)/shard_map/reshape | solution.py:57
  118.0 3.2 %gather_fusion.1 = bf16[32,128,128]{2,1,0:T(8,128)(2,1)} fusion(bf16[128,64,128]{2,0,1:T(8,128)(2,1)} %copy.49, s32[1024]{0:T(1024)S(1)} %pad_clamp_fusion), kind=kCustom, calls=%fused_computation.1.clone | custom fusion | bytes 2097280 | tf_op jit(solution)/shard_map/jit(_take)/gather | solution.py:57
  124.2 1.8 fusion.30
  126.0 2.5 broadcast_in_dim.14.clone.1
  128.4 7.0 %scatter_fusion.1 = f32[128,64,128]{2,0,1:T(8,128)} fusion(f32[128,64,128]{2,0,1:T(8,128)} %broadcast_in_dim.14.clone.1, s32[32]{0:T(128)S(1)} %fusion.26, f32[32,128,128]{2,1,0:T(8,128)} %bitcast.146), kind=kCustom, calls=%fused_computation.3 | custom fusion | flops 524288 | bytes 6291584 | tf_op jit(solution)/shard_map/scatter-add | solution.py:63
  135.4 5.6 %copy.50 = f32[128,64,128]{0,2,1:T(8,128)} copy(f32[128,64,128]{2,0,1:T(8,128)} %scatter_fusion.1) | data formatting | bytes 8388608 | tf_op jit(solution)/shard_map/scatter-add | solution.py:63
  141.0 1.8 fusion.24
  142.9 1.7 fusion.23
  144.6 1.7 fusion.22
  146.3 1.7 fusion.21
  147.9 1.7 fusion.20
  149.6 1.7 fusion.19
  151.3 1.7 fusion.18
  152.9 1.7 fusion.17
  160.3 20.8 %all-to-all-done = f32[128,16,512]{0,2,1:T(8,128)} async-done(((f32[128,16,512]{0,2,1:T(8,128)}), f32[128,16,512]{0,2,1:T(8,128)}, u32[]{:S(2)}, u32[]{:S(2)}) %all-to-all-start) | async-done | bytes 4194336 | tf_op jit(solution)/shard_map/all_to_all | solution.py:56
  181.1 5.0 %all-to-all-start.1 = ((f32[16,128,512]{1,2,0:T(8,128)}), f32[16,128,512]{1,2,0:T(8,128)}, u32[]{:S(2)}, u32[]{:S(2)}) async-start(f32[16,128,512]{1,2,0:T(8,128)} %fusion.9), calls=%async_computation.1 | async-start | bytes 8388608 | tf_op jit(solution)/shard_map/all_to_all | solution.py:14
  187.6 2.7 fusion
  190.3 63.8 %all-reduce.3.cloned.1.call-done = (bf16[8,4,128,128]{3,2,1,0:T(8,128)(2,1)}, bf16[8,4,128,128]{2,3,1,0:T(8,128)(2,1)}) async-done(((bf16[8,4,128,128]{3,2,1,0:T(8,128)(2,1)}, bf16[8,4,128,128]{2,3,1,0:T(8,128)(2,1)}), (bf16[8,4,128,128]{3,2,1,0:T(8,128)(2,1)}, bf16[8,4,128,128]{2,3,1,0:T(8,128)(2,1)})) %all-reduce.3.cloned.1.call-update) | async-done | bytes 2097168 | tf_op jit(solution)/shard_map/psum | solution.py:69
  254.2 2.3 copy.55
  256.4 2.5 reduce_sum.18
  259.7 18.9 %all-to-all-done.1 = f32[16,128,512]{1,2,0:T(8,128)} async-done(((f32[16,128,512]{1,2,0:T(8,128)}), f32[16,128,512]{1,2,0:T(8,128)}, u32[]{:S(2)}, u32[]{:S(2)}) %all-to-all-start.1) | async-done | bytes 4194336 | tf_op jit(solution)/shard_map/all_to_all | solution.py:14
  278.6 2.4 reduce_sum.19
  (47 shorter events, 19.4 us)
Async XLA Ops:
  7.2 52.6 %copy-start = (bf16[8,4,128,128]{3,2,1,0:T(8,128)(2,1)S(1)}, bf16[8,4,128,128]{3,2,1,0:T(8,128)(2,1)}, u32[]{:S(2)}) copy-start(bf16[8,4,128,128]{3,2,1,0:T(8,128)(2,1)} %param.12) | copy-start | bytes 3145732
  7.2 44.7 %all-gather.3.cloned.1.call-start = ((), (), s32[]{:S(2)}) async-start(), calls=%async_computation.2 | async-start | bytes 2228224 | tf_op jit(solution)/shard_map/all_gather | solution.py:37
  9.0 104.9 %all-gather.5.cloned.1.call-start = ((), (), s32[]{:S(2)}) async-start(), calls=%async_computation.3 | async-start | bytes 2228224 | tf_op jit(solution)/shard_map/all_gather | solution.py:38
  76.6 104.5 %all-to-all-start = ((f32[128,16,512]{0,2,1:T(8,128)}), f32[128,16,512]{0,2,1:T(8,128)}, u32[]{:S(2)}, u32[]{:S(2)}) async-start(f32[128,16,512]{0,2,1:T(8,128)} %bitcast.142), calls=%async_computation | async-start | bytes 8388608 | tf_op jit(solution)/shard_map/all_to_all | solution.py:56
  121.2 2.9 %copy-start.3 = (bf16[8,4,128,128]{3,2,1,0:T(8,128)(2,1)S(1)}, bf16[8,4,128,128]{3,2,1,0:T(8,128)(2,1)}, u32[]{:S(2)}) copy-start(bf16[8,4,128,128]{3,2,1,0:T(8,128)(2,1)} %param.10) | copy-start | bytes 3145732
  122.7 1.0 copy-start.2
  141.0 13.5 %copy-start.1 = (f32[128,64,128]{0,2,1:T(8,128)S(1)}, f32[128,64,128]{0,2,1:T(8,128)}, u32[]{:S(2)}) copy-start(f32[128,64,128]{0,2,1:T(8,128)} %copy.50) | copy-start | bytes 12582916
  181.1 97.4 %all-to-all-start.1 = ((f32[16,128,512]{1,2,0:T(8,128)}), f32[16,128,512]{1,2,0:T(8,128)}, u32[]{:S(2)}, u32[]{:S(2)}) async-start(f32[16,128,512]{1,2,0:T(8,128)} %fusion.9), calls=%async_computation.1 | async-start | bytes 8388608 | tf_op jit(solution)/shard_map/all_to_all | solution.py:14
  186.1 68.1 %all-reduce.3.cloned.1.call-start = ((), (), s32[]{:S(2)}) async-start(), calls=%async_computation.4 | async-start | bytes 4194304 | tf_op jit(solution)/shard_map/psum | solution.py:69
  256.4 25.3 %copy-start.4 = (bf16[8,4,128,128]{3,2,1,0:T(8,128)(2,1)S(1)}, bf16[8,4,128,128]{3,2,1,0:T(8,128)(2,1)}, u32[]{:S(2)}) copy-start(bf16[8,4,128,128]{3,2,1,0:T(8,128)(2,1)} %get-tuple-element.25) | copy-start | bytes 3145732
Sparse Core Ops, SparseCore 0:
  10.8 41.0 all-gather.2
  54.6 59.2 all-gather.4
  190.5 63.6 all-reduce.2
